TPU v7x, 512 devices: a whole 4x4x16 slice. The times are simulated.
512 devices in a mesh: dp: 16 (over y, z_lo), page: 32 (over z_hi, x, core).
Axes of the slice: x: 4, y: 4, z: 16 (z_hi: 4, z_lo: 4; z = z_hi * 4 + z_lo), core: 2. Of those that a mesh axis runs over, the one named last changes fastest.
Arguments:
- queries: bfloat16 [16, 32, 128, 1024], P('dp', 'page'), may hold values from -200 to 200
- keys: bfloat16 [16, 32, 128, 1024], P('dp', 'page'), may hold values from -6 to 6
- values: bfloat16 [16, 32, 128, 1024], P('dp', 'page'), may hold values from -6 to 6
- grad_out: bfloat16 [16, 32, 128, 1024], P('dp', 'page'), may hold values from -6 to 6
- out_weight: bfloat16 [1024, 1024], P(('dp', 'page')), may hold values from -0.1875 to 0.1875
- partners: int32 [16, 2, 32], P('dp'), may hold values from 0 to 31, as said below
- block_mask: int32 [16, 32, 2, 1, 1], P('dp', 'page'), may hold values 0 or 1
- buckets: int32 [16, 32, 3, 1, 1], P('dp', 'page'), may hold values from 0 to 31
- bias_table: float32 [32, 16], replicated, may hold values from -4 to 4
Outputs:
- layer_out: bfloat16 [16, 32, 128, 1024], P('dp', 'page')
- query_grad: bfloat16 [16, 32, 128, 1024], P('dp', 'page')
- key_grad: bfloat16 [16, 32, 128, 1024], P('dp', 'page')
- value_grad: bfloat16 [16, 32, 128, 1024], P('dp', 'page')
- weight_grad: float32 [1024, 1024], P(('dp', 'page'))
Inputs may be any that keep to these rules, and one draw needn't show every extreme that they name: partners[f, r, partners[f, r, p]] = p and partners[f, r, p] != p.
All inputs are finite; a program needn't handle non-finite values. No bound on the sum of `block_mask` on one device may be relied on, other than what follows from the above.
Results may differ from a plain program's by a relative error of at most 0.025.
Values may be sent and summed in bfloat16 or wider, within the bound.
No kernel may reach another device: no remote copies, remote signals or barrier semaphores. Data moves between devices by JAX's collectives and lax.ppermute only.
A program may use at most 64 MiB of HBM per device.

v0:
```python
import math
import jax
import jax.numpy as jnp
from jax import lax
from jax.sharding import PartitionSpec as P

H = 16
BLOCK = 128
ROUNDS = 2
heads_per_step = 4
neg_large = -1e30


def head_steps(query_rows, key_set, value_set, grad_rows, bias_blocks, allowed):
    page_len, width = query_rows.shape
    key_count = key_set.shape[0]
    groups = key_count // page_len
    head_dim = width // H
    step_count = H // heads_per_step
    block_count = page_len // BLOCK
    scale = 1.0 / math.sqrt(head_dim)

    def split(array):
        return array.reshape(array.shape[0], step_count, heads_per_step, head_dim).transpose(
            1, 0, 2, 3
        )

    bias_split = bias_blocks.reshape(
        groups, block_count, block_count, step_count, heads_per_step
    ).transpose(3, 4, 1, 0, 2)
    allow_wide = allowed.transpose(1, 0, 2)[None, :, None, :, :, None]

    def one_step(inputs):
        q_part, k_part, v_part, g_part, b_part = inputs
        scores = (
            jnp.einsum("qhd,khd->hqk", q_part, k_part, preferred_element_type=jnp.float32) * scale
        )
        scores = scores.reshape(heads_per_step, block_count, BLOCK, groups, block_count, BLOCK)
        scores = scores + b_part[:, :, None, :, :, None]
        scores = jnp.where(allow_wide, scores, neg_large).reshape(
            heads_per_step, page_len, key_count
        )
        top = jnp.max(scores, axis=-1, keepdims=True)
        expo = jnp.exp(scores - top)
        prob = expo / jnp.sum(expo, axis=-1, keepdims=True)
        prob_b = prob.astype(jnp.bfloat16)
        attn_part = jnp.einsum(
            "hqk,khd->qhd", prob_b, v_part, preferred_element_type=jnp.float32
        ).astype(jnp.bfloat16)
        dprob = jnp.einsum("qhd,khd->hqk", g_part, v_part, preferred_element_type=jnp.float32)
        row_dot = jnp.sum(g_part.astype(jnp.float32) * attn_part.astype(jnp.float32), axis=-1).T[
            :, :, None
        ]
        dscore = (prob * (dprob - row_dot) * scale).astype(jnp.bfloat16)
        q_grad = jnp.einsum("hqk,khd->qhd", dscore, k_part, preferred_element_type=jnp.float32)
        k_grad = jnp.einsum("hqk,qhd->khd", dscore, q_part, preferred_element_type=jnp.float32)
        v_grad = jnp.einsum("hqk,qhd->khd", prob_b, g_part, preferred_element_type=jnp.float32)
        return (attn_part, q_grad, k_grad, v_grad)

    results = lax.map(
        one_step,
        (split(query_rows), split(key_set), split(value_set), split(grad_rows), bias_split),
    )

    def join(array):
        return array.transpose(1, 0, 2, 3).reshape(array.shape[1], width)

    return (join(results[0]), join(results[1]), join(results[2]), join(results[3]))


def shards(queries, keys, values, grad_out, out_weight, partners, block_mask, buckets, bias_table):
    weight = lax.all_gather(out_weight, ("dp", "page"), axis=0, tiled=True)
    q_page = queries[0, 0]
    k_page = keys[0, 0]
    v_page = values[0, 0]
    g_page = grad_out[0, 0]
    page_len, width = q_page.shape
    block_count = page_len // BLOCK
    peers = lax.axis_size("page")
    piece_rows = page_len // peers
    mates = partners[0]
    kv_pair = jnp.stack([k_page, v_page])
    d_attn = lax.dot_general(
        g_page, weight, (((1,), (1,)), ((), ())), preferred_element_type=jnp.float32
    ).astype(jnp.bfloat16)

    def spread(stacked):
        pieces = stacked.reshape(2, peers, piece_rows, width)
        return lax.all_to_all(pieces, "page", split_axis=1, concat_axis=1, tiled=True)

    def collect(received, chosen):
        picked = jnp.take(received, chosen, axis=1)
        back = lax.all_to_all(picked, "page", split_axis=2, concat_axis=2, tiled=True)
        return back.reshape(2, chosen.shape[0], page_len, width)

    fetched = jnp.concatenate(
        [collect(spread(kv_pair), mates[r : r + 1]) for r in range(ROUNDS)], 1
    )
    key_set = jnp.concatenate([k_page[None], fetched[0]], 0).reshape(-1, width)
    value_set = jnp.concatenate([v_page[None], fetched[1]], 0).reshape(-1, width)
    bucket_ids = buckets[0, 0]
    one_hot = bucket_ids[..., None] == jnp.arange(bias_table.shape[0], dtype=jnp.int32)
    bias_blocks = jnp.sum(jnp.where(one_hot[..., None], bias_table, 0.0), axis=-2)
    allowed = jnp.concatenate(
        [jnp.ones((1, block_count, block_count), bool), block_mask[0, 0] == 1], 0
    )
    attn, q_grad, k_grad, v_grad = head_steps(
        q_page, key_set, value_set, d_attn, bias_blocks, allowed
    )
    layer_out = jnp.dot(attn, weight, preferred_element_type=jnp.float32).astype(jnp.bfloat16)
    weight_grad = lax.psum_scatter(
        lax.dot_general(attn, g_page, (((0,), (0,)), ((), ())), preferred_element_type=jnp.float32),
        ("dp", "page"),
        scatter_dimension=0,
        tiled=True,
    )
    outgoing = (
        jnp.stack([k_grad[page_len:], v_grad[page_len:]])
        .reshape(2, ROUNDS, page_len, width)
        .astype(jnp.bfloat16)
    )

    def give_back(terms, chosen):
        round_count = terms.shape[1]
        pieces = terms.reshape(2, round_count, peers, piece_rows, width)
        received = lax.all_to_all(pieces, "page", split_axis=2, concat_axis=2, tiled=True)
        picked = jnp.stack([jnp.take(received[:, 0], chosen[0], axis=1)], 1)
        back = lax.all_to_all(picked, "page", split_axis=2, concat_axis=2, tiled=True)
        return back.reshape(2, round_count, page_len, width)

    returned = jnp.concatenate(
        [give_back(outgoing[:, r : r + 1], mates[r : r + 1]) for r in range(ROUNDS)], 1
    )
    totals = jnp.stack([k_grad[:page_len], v_grad[:page_len]]) + jnp.sum(
        returned.astype(jnp.float32), axis=1
    )
    key_grad = totals[0].astype(jnp.bfloat16)[None, None]
    value_grad = totals[1].astype(jnp.bfloat16)[None, None]
    return (
        layer_out[None, None],
        q_grad.astype(jnp.bfloat16)[None, None],
        key_grad,
        value_grad,
        weight_grad,
    )


def solution(mesh):
    in_specs = (
        P("dp", "page", None, None),
        P("dp", "page", None, None),
        P("dp", "page", None, None),
        P("dp", "page", None, None),
        P(("dp", "page"), None),
        P("dp", None, None),
        P("dp", "page", None, None, None),
        P("dp", "page", None, None, None),
        P(),
    )
    out_specs = (
        P("dp", "page", None, None),
        P("dp", "page", None, None),
        P("dp", "page", None, None),
        P("dp", "page", None, None),
        P(("dp", "page"), None),
    )
    return jax.shard_map(shards, mesh=mesh, in_specs=in_specs, out_specs=out_specs, check_vma=False)
```

profile of v0, /device:TPU:2, one launch (start us, length us, event | category | flops | bytes accessed | tf_op | source)
XLA Modules:
  0.0 1547.2 jit_solution(18248375689373877247)
XLA Ops:
  10.5 18.2 %all-to-all-start = ((bf16[2,32,4,1024]{3,2,0,1:T(4,128)(2,1)}), bf16[2,32,4,1024]{3,2,0,1:T(4,128)(2,1)S(1)}, u32[]{:S(2)}, u32[]{:S(2)}) async-start(bf16[2,32,4,1024]{3,2,0,1:T(4,128)(2,1)} %pad_maximum_fusion.4), calls=%async_computation | async-start | bytes 1048576 | tf_op jit(solution)/shard_map/all_to_all | solution.py:89
  28.8 27.8 %all-to-all-done = bf16[2,32,4,1024]{3,2,0,1:T(4,128)(2,1)S(1)} async-done(((bf16[2,32,4,1024]{3,2,0,1:T(4,128)(2,1)}), bf16[2,32,4,1024]{3,2,0,1:T(4,128)(2,1)S(1)}, u32[]{:S(2)}, u32[]{:S(2)}) %all-to-all-start) | async-done | bytes 524320 | tf_op jit(solution)/shard_map/all_to_all | solution.py:89
  58.9 10.8 all-to-all-start.1
  72.7 25.7 %all-to-all-done.1 = bf16[2,1,32,4,1024]{4,3,0,1,2:T(4,128)(2,1)S(1)} async-done(((bf16[2,1,32,4,1024]{4,3,0,1,2:T(4,128)(2,1)}), bf16[2,1,32,4,1024]{4,3,0,1,2:T(4,128)(2,1)S(1)}, u32[]{:S(2)}, u32[]{:S(2)}) %all-to-all-start.1) | async-done | bytes 524320 | tf_op jit(solution)/shard_map/all_to_all | solution.py:93
  98.4 10.6 all-to-all-start.2
  111.2 25.7 %all-to-all-done.2 = bf16[2,1,32,4,1024]{4,3,0,1,2:T(4,128)(2,1)S(1)} async-done(((bf16[2,1,32,4,1024]{4,3,0,1,2:T(4,128)(2,1)}), bf16[2,1,32,4,1024]{4,3,0,1,2:T(4,128)(2,1)S(1)}, u32[]{:S(2)}, u32[]{:S(2)}) %all-to-all-start.2) | async-done | bytes 524320 | tf_op jit(solution)/shard_map/all_to_all | solution.py:93
  144.2 712.5 %all-gather.3.cloned.1.call-done = bf16[512,2,1024]{2,1,0:T(2,128)(2,1)} async-done(((bf16[1,2,1024]{2,1,0:T(2,128)(2,1)}), bf16[512,2,1024]{2,1,0:T(2,128)(2,1)}) %all-gather.3.cloned.1.call-update) | async-done | bytes 2097168 | tf_op jit(solution)/shard_map/all_gather | solution.py:72
  856.7 2.7 reshape.233
  861.2 50.1 %while.16 = (s32[]{:T(128)}, bf16[4,128,4,64]{1,3,2,0:T(8,128)(2,1)}, bf16[4,128,4,64]{1,3,2,0:T(8,128)(2,1)}, f32[4,384,4,64]{1,3,2,0:T(8,128)}, f32[4,384,4,64...) while((s32[]{:T(128)}, ...), condition=%wide.region_5.7_spmd, body=%wide.region_1.6_spmd.sunk | while | flops 205817472 | bytes 5562152 | solution.py:60
  870.6 2.2 fusion.130
  883.1 2.3 fusion.130
  895.6 2.2 fusion.130
  913.5 2.7 copy.125
  920.3 3.8 copy.126
  924.1 3.9 fusion.69
  929.1 8.3 all-to-all-start.3
  938.5 27.1 %all-to-all-done.3 = bf16[2,1,32,4,1024]{4,3,0,1,2:T(4,128)(2,1)S(1)} async-done(((bf16[2,1,32,4,1024]{4,3,0,1,2:T(4,128)(2,1)}), bf16[2,1,32,4,1024]{4,3,0,1,2:T(4,128)(2,1)S(1)}, u32[]{:S(2)}, u32[]{:S(2)}) %all-to-all-start.3) | async-done | bytes 524320 | tf_op jit(solution)/shard_map/all_to_all | solution.py:126
  965.6 10.5 all-to-all-start.5
  980.3 24.5 %all-to-all-done.5 = bf16[2,1,32,4,1024]{4,3,0,1,2:T(4,128)(2,1)S(1)} async-done(((bf16[2,1,32,4,1024]{4,3,0,1,2:T(4,128)(2,1)}), bf16[2,1,32,4,1024]{4,3,0,1,2:T(4,128)(2,1)S(1)}, u32[]{:S(2)}, u32[]{:S(2)}) %all-to-all-start.5) | async-done | bytes 524320 | tf_op jit(solution)/shard_map/all_to_all | solution.py:126
  1004.8 10.4 all-to-all-start.4
  1015.5 3.6 fusion.72
  1023.2 20.7 %all-to-all-done.4 = bf16[2,1,32,4,1024]{4,3,0,1,2:T(4,128)(2,1)S(1)} async-done(((bf16[2,1,32,4,1024]{4,3,0,1,2:T(4,128)(2,1)}), bf16[2,1,32,4,1024]{4,3,0,1,2:T(4,128)(2,1)S(1)}, u32[]{:S(2)}, u32[]{:S(2)}) %all-to-all-start.4) | async-done | bytes 524320 | tf_op jit(solution)/shard_map/all_to_all | solution.py:128
  1044.0 10.6 all-to-all-start.6
  1063.3 467.6 %all-reduce.3.cloned.1.call-done = f32[1024,1024]{1,0:T(8,128)} async-done(((f32[1024,1024]{1,0:T(8,128)}), f32[1024,1024]{1,0:T(8,128)}) %all-reduce.3.cloned.1.call-update) | async-done | bytes 4194320
  (147 shorter events, 97.8 us)
Async XLA Ops:
  7.2 852.3 %copy-start = (bf16[1,1,128,1024]{3,2,1,0:T(8,128)(2,1)S(1)}, bf16[1,1,128,1024]{3,2,1,0:T(8,128)(2,1)}, u32[]{:S(2)}) copy-start(bf16[1,1,128,1024]{3,2,1,0:T(8,128)(2,1)} %param.18) | copy-start | bytes 786436
  7.2 21.6 %copy-start.6 = (s32[1,2,32]{2,1,0:T(2,128)S(1)}, s32[1,2,32]{2,1,0:T(2,128)}, u32[]{:S(2)}) copy-start(s32[1,2,32]{2,1,0:T(2,128)} %param.20) | copy-start | bytes 772
  10.5 46.2 %all-to-all-start = ((bf16[2,32,4,1024]{3,2,0,1:T(4,128)(2,1)}), bf16[2,32,4,1024]{3,2,0,1:T(4,128)(2,1)S(1)}, u32[]{:S(2)}, u32[]{:S(2)}) async-start(bf16[2,32,4,1024]{3,2,0,1:T(4,128)(2,1)} %pad_maximum_fusion.4), calls=%async_computation | async-start | bytes 1048576 | tf_op jit(solution)/shard_map/all_to_all | solution.py:89
  58.9 39.4 %all-to-all-start.1 = ((bf16[2,1,32,4,1024]{4,3,0,1,2:T(4,128)(2,1)}), bf16[2,1,32,4,1024]{4,3,0,1,2:T(4,128)(2,1)S(1)}, u32[]{:S(2)}, u32[]{:S(2)}) async-start(bf16[2,1,32,4,1024]{4,3,0,1,2:T(4,128)(2,1)} %fusion.71), calls=%async_computation.1 | async-start | bytes 1048576 | tf_op jit(solution)/shard_map/all_to_all | solution.py:93
  69.8 786.9 %all-gather.3.cloned.1.call-start = ((), (), s32[]{:S(2)}) async-start(), calls=%async_computation.7 | async-start | bytes 2101248 | tf_op jit(solution)/shard_map/all_gather | solution.py:72
  70.5 38.5 %copy-start.5 = (bf16[1,1,128,1024]{3,2,1,0:T(8,128)(2,1)S(1)}, bf16[1,1,128,1024]{3,2,1,0:T(8,128)(2,1)}, u32[]{:S(2)}) copy-start(bf16[1,1,128,1024]{3,2,1,0:T(8,128)(2,1)} %param.15) | copy-start | bytes 786436
  71.5 38.3 %copy-start.9 = (s32[1,1,3,1,1]{2,4,3,1,0:T(1,128)S(1)}, s32[1,1,3,1,1]{2,4,3,1,0:T(1,128)}, u32[]{:S(2)}) copy-start(s32[1,1,3,1,1]{2,4,3,1,0:T(1,128)} %param.22) | copy-start | bytes 40
  71.6 38.4 %copy-start.8 = (f32[32,16]{0,1:T(8,128)S(1)}, f32[32,16]{0,1:T(8,128)}, u32[]{:S(2)}) copy-start(f32[32,16]{0,1:T(8,128)} %param.23) | copy-start | bytes 6148
  71.6 38.5 %copy-start.10 = (s32[1,1,2,1,1]{2,4,3,1,0:T(1,128)S(1)}, s32[1,1,2,1,1]{2,4,3,1,0:T(1,128)}, u32[]{:S(2)}) copy-start(s32[1,1,2,1,1]{2,4,3,1,0:T(1,128)} %param.21) | copy-start | bytes 28
  98.4 38.5 %all-to-all-start.2 = ((bf16[2,1,32,4,1024]{4,3,0,1,2:T(4,128)(2,1)}), bf16[2,1,32,4,1024]{4,3,0,1,2:T(4,128)(2,1)S(1)}, u32[]{:S(2)}, u32[]{:S(2)}) async-start(bf16[2,1,32,4,1024]{4,3,0,1,2:T(4,128)(2,1)} %fusion.70), calls=%async_computation.2 | async-start | bytes 1048576 | tf_op jit(solution)/shard_map/all_to_all | solution.py:93
  861.9 4.3 copy-start.11
  864.1 2.2 copy-start.12
  874.5 4.3 copy-start.11
  887.0 4.3 copy-start.11
  889.2 2.2 copy-start.12
  899.5 4.3 copy-start.11
  928.0 9.4 copy-start.2
  929.1 47.0 %copy-start.7 = (s32[1,2,32]{2,1,0:T(2,128)S(1)}, s32[1,2,32]{2,1,0:T(2,128)}, u32[]{:S(2)}) copy-start(s32[1,2,32]{2,1,0:T(2,128)} %param.20) | copy-start | bytes 772
  929.1 36.5 %all-to-all-start.3 = ((bf16[2,1,32,4,1024]{4,3,0,1,2:T(4,128)(2,1)}), bf16[2,1,32,4,1024]{4,3,0,1,2:T(4,128)(2,1)S(1)}, u32[]{:S(2)}, u32[]{:S(2)}) async-start(bf16[2,1,32,4,1024]{4,3,0,1,2:T(4,128)(2,1)} %copy.127), calls=%async_computation.3 | async-start | bytes 1048576 | tf_op jit(solution)/shard_map/all_to_all | solution.py:126
  965.6 39.2 %all-to-all-start.5 = ((bf16[2,1,32,4,1024]{4,3,0,1,2:T(4,128)(2,1)}), bf16[2,1,32,4,1024]{4,3,0,1,2:T(4,128)(2,1)S(1)}, u32[]{:S(2)}, u32[]{:S(2)}) async-start(bf16[2,1,32,4,1024]{4,3,0,1,2:T(4,128)(2,1)} %copy.131), calls=%async_computation.5 | async-start | bytes 1048576 | tf_op jit(solution)/shard_map/all_to_all | solution.py:126
  1004.8 39.2 %all-to-all-start.4 = ((bf16[2,1,32,4,1024]{4,3,0,1,2:T(4,128)(2,1)}), bf16[2,1,32,4,1024]{4,3,0,1,2:T(4,128)(2,1)S(1)}, u32[]{:S(2)}, u32[]{:S(2)}) async-start(bf16[2,1,32,4,1024]{4,3,0,1,2:T(4,128)(2,1)} %select_bitcast_fusion.1), calls=%async_computation.4 | async-start | bytes 1048576 | tf_op jit(solution)/shard_map/all_to_all | solution.py:128
  1015.2 515.7 %all-reduce.3.cloned.1.call-start = ((), (), s32[]{:S(2)}) async-start(), calls=%async_computation.8 | async-start | bytes 8388608
  1044.0 13.7 copy-start.1
  1044.0 489.9 %all-to-all-start.6 = ((bf16[2,1,32,4,1024]{4,3,0,1,2:T(4,128)(2,1)}), bf16[2,1,32,4,1024]{4,3,0,1,2:T(4,128)(2,1)}, u32[]{:S(2)}, u32[]{:S(2)}) async-start(bf16[2,1,32,4,1024]{4,3,0,1,2:T(4,128)(2,1)} %select_bitcast_fusion), calls=%async_computation.6 | async-start | bytes 1048576 | tf_op jit(solution)/shard_map/all_to_all | solution.py:128
  (4 other events, 7.0 us)
Sparse Core Ops, SparseCore 0:
  72.7 783.9 all-gather.2
  1021.4 509.4 all-reduce.2
where the time goes:
time: 1550 us
  waiting for transfers between devices  1330 us (86%)
  starting transfers between devices  79.8 us (5%)
  local copies, waits for them, and re-layouts  51.8 us (3%)
  matrix products  50.2 us (3%)
  other arithmetic  18.3 us (1%)
    all_gather x1, waiting for transfers between devices, shards(): weight = lax.all_gather(out_weight, ('dp', 'page'), axis=0, tiled=True)  713 us
    unnamed x3, waiting for transfers between devices  468 us
    all_to_all x2, waiting for transfers between devices, give_back(): lax.all_to_all(pieces, 'page', split_axis=2, concat_axis=2, tiled=True)  51.6 us
    all_to_all x2, waiting for transfers between devices, collect(): lax.all_to_all(picked, 'page', split_axis=2, concat_axis=2, tiled=True)  51.4 us
  transfers between devices with their start and end apart: 9, of which 8 were waited for; matrix products, arithmetic and copies ran while one was open for 2% of the time, Pallas kernels for 0%

commit v1 on v0

--- a/solution.py
+++ b/solution.py
@@ -123,7 +123,10 @@
     def give_back(terms, chosen):
         round_count = terms.shape[1]
         pieces = terms.reshape(2, round_count, peers, piece_rows, width)
-        received = lax.all_to_all(pieces, "page", split_axis=2, concat_axis=2, tiled=True)
+        size = lax.axis_size("page")
+        blocks = jnp.stack(jnp.split(pieces, size, axis=2), axis=0)
+        blocks = lax.all_to_all(blocks, "page", split_axis=0, concat_axis=0)
+        received = jnp.concatenate(blocks, axis=2)
         picked = jnp.stack([jnp.take(received[:, 0], chosen[0], axis=1)], 1)
         back = lax.all_to_all(picked, "page", split_axis=2, concat_axis=2, tiled=True)
         return back.reshape(2, round_count, page_len, width)

time: 1550 us -> 1570 us (1.013)
  local copies, waits for them, and re-layouts: 51.8 us -> 84.5 us
  waiting for transfers between devices: 1330 us -> 1310 us
    unnamed x30 -> x92, local copies, waits for them, and re-layouts: 9.48 us -> 47.4 us
    all_to_all x2, waiting for transfers between devices: 51.6 us -> 32.7 us  [give_back(): blocks = lax.all_to_all(blocks, 'page', split_axis=0, concat_axis=0)]
  transfers between devices with their start and end apart: 9 -> 9, of which waited for: 8 -> 8; matrix products, arithmetic and copies ran while one was open for 2% -> 3% of each run, Pallas kernels for 0% -> 0%
where the time goes in v1:
time: 1570 us; the launch traced here: 1560 us
  waiting for transfers between devices  1310 us (83%)
  local copies, waits for them, and re-layouts  84.5 us (5%)
  starting transfers between devices  79.6 us (5%)
  matrix products  50.2 us (3%)
  other arithmetic  22.7 us (1%)
    all_gather x1, waiting for transfers between devices, shards(): weight = lax.all_gather(out_weight, ('dp', 'page'), axis=0, tiled=True)  713 us
    unnamed x3, waiting for transfers between devices  469 us
    all_to_all x2, waiting for transfers between devices, collect(): lax.all_to_all(picked, 'page', split_axis=2, concat_axis=2, tiled=True)  51.4 us
    unnamed x92, local copies, waits for them, and re-layouts  47.4 us
    all_to_all x2, waiting for transfers between devices, give_back(): blocks = lax.all_to_all(blocks, 'page', split_axis=0, concat_axis=0)  32.7 us
  transfers between devices with their start and end apart: 9, of which 8 were waited for; matrix products, arithmetic and copies ran while one was open for 3% of the time, Pallas kernels for 0%

profile of v1, /device:TPU:2, one launch (start us, length us, event | category | flops | bytes accessed | tf_op | source)
XLA Modules:
  0.0 1564.4 jit_solution(8226999290201410836)
XLA Ops:
  10.5 18.2 %all-to-all-start = ((bf16[2,32,4,1024]{3,2,0,1:T(4,128)(2,1)}), bf16[2,32,4,1024]{3,2,0,1:T(4,128)(2,1)S(1)}, u32[]{:S(2)}, u32[]{:S(2)}) async-start(bf16[2,32,4,1024]{3,2,0,1:T(4,128)(2,1)} %pad_maximum_fusion.4), calls=%async_computation | async-start | bytes 1048576 | tf_op jit(solution)/shard_map/all_to_all | solution.py:89
  28.8 27.8 %all-to-all-done = bf16[2,32,4,1024]{3,2,0,1:T(4,128)(2,1)S(1)} async-done(((bf16[2,32,4,1024]{3,2,0,1:T(4,128)(2,1)}), bf16[2,32,4,1024]{3,2,0,1:T(4,128)(2,1)S(1)}, u32[]{:S(2)}, u32[]{:S(2)}) %all-to-all-start) | async-done | bytes 524320 | tf_op jit(solution)/shard_map/all_to_all | solution.py:89
  58.9 10.8 all-to-all-start.1
  72.7 25.7 %all-to-all-done.1 = bf16[2,1,32,4,1024]{4,3,0,1,2:T(4,128)(2,1)S(1)} async-done(((bf16[2,1,32,4,1024]{4,3,0,1,2:T(4,128)(2,1)}), bf16[2,1,32,4,1024]{4,3,0,1,2:T(4,128)(2,1)S(1)}, u32[]{:S(2)}, u32[]{:S(2)}) %all-to-all-start.1) | async-done | bytes 524320 | tf_op jit(solution)/shard_map/all_to_all | solution.py:93
  98.4 10.6 all-to-all-start.2
  111.2 25.7 %all-to-all-done.2 = bf16[2,1,32,4,1024]{4,3,0,1,2:T(4,128)(2,1)S(1)} async-done(((bf16[2,1,32,4,1024]{4,3,0,1,2:T(4,128)(2,1)}), bf16[2,1,32,4,1024]{4,3,0,1,2:T(4,128)(2,1)S(1)}, u32[]{:S(2)}, u32[]{:S(2)}) %all-to-all-start.2) | async-done | bytes 524320 | tf_op jit(solution)/shard_map/all_to_all | solution.py:93
  144.2 712.5 %all-gather.3.cloned.1.call-done = bf16[512,2,1024]{2,1,0:T(2,128)(2,1)} async-done(((bf16[1,2,1024]{2,1,0:T(2,128)(2,1)}), bf16[512,2,1024]{2,1,0:T(2,128)(2,1)}) %all-gather.3.cloned.1.call-update) | async-done | bytes 2097168 | tf_op jit(solution)/shard_map/all_gather | solution.py:72
  856.7 2.7 reshape.241
  861.2 50.1 %while.16 = (s32[]{:T(128)}, bf16[4,128,4,64]{1,3,2,0:T(8,128)(2,1)}, bf16[4,128,4,64]{1,3,2,0:T(8,128)(2,1)}, f32[4,384,4,64]{1,3,2,0:T(8,128)}, f32[4,384,4,64...) while((s32[]{:T(128)}, ...), condition=%wide.region_5.7_spmd, body=%wide.region_1.6_spmd.sunk | while | flops 205817472 | bytes 5562152 | solution.py:60
  913.5 2.7 copy.183
  920.3 3.8 copy.184
  924.1 3.9 fusion.69
  947.6 8.3 all-to-all-start.3
  975.5 8.7 all-to-all-done.3
  984.2 10.5 all-to-all-start.5
  999.5 23.9 %all-to-all-done.5 = bf16[32,2,1,1,4,1024]{5,1,4,3,2,0:T(2,128)(2,1)S(1)} async-done(((bf16[32,2,1,1,4,1024]{5,1,4,3,2,0:T(2,128)(2,1)}), bf16[32,2,1,1,4,1024]{5,1,4,3,2,0:T(2,128)(2,1)S(1)}, u32[]{:S(2)}, u32[]{:S(2)}) %all-to-all-start.5) | async-done | bytes 524320 | tf_op jit(solution)/shard_map/all_to_all | solution.py:128
  1023.4 10.3 all-to-all-start.4
  1033.8 3.6 fusion.74
  1037.4 2.4 gather_fusion.3
  1039.8 2.5 fusion.73
  1042.3 19.7 %all-to-all-done.4 = bf16[2,1,32,4,1024]{4,0,3,1,2:T(2,128)(2,1)S(1)} async-done(((bf16[2,1,32,4,1024]{4,0,3,1,2:T(2,128)(2,1)}), bf16[2,1,32,4,1024]{4,0,3,1,2:T(2,128)(2,1)S(1)}, u32[]{:S(2)}, u32[]{:S(2)}) %all-to-all-start.4) | async-done | bytes 524320 | tf_op jit(solution)/shard_map/all_to_all | solution.py:131
  1062.0 10.9 all-to-all-start.6
  1081.6 468.0 %all-reduce.3.cloned.1.call-done = f32[1024,1024]{1,0:T(8,128)} async-done(((f32[1024,1024]{1,0:T(8,128)}), f32[1024,1024]{1,0:T(8,128)}) %all-reduce.3.cloned.1.call-update) | async-done | bytes 4194320
  1551.0 3.2 convert_reduce_fusion
  (205 shorter events, 133.3 us)
Async XLA Ops:
  7.2 852.3 %copy-start = (bf16[1,1,128,1024]{3,2,1,0:T(8,128)(2,1)S(1)}, bf16[1,1,128,1024]{3,2,1,0:T(8,128)(2,1)}, u32[]{:S(2)}) copy-start(bf16[1,1,128,1024]{3,2,1,0:T(8,128)(2,1)} %param.18) | copy-start | bytes 786436
  7.2 21.6 %copy-start.6 = (s32[1,2,32]{2,1,0:T(2,128)S(1)}, s32[1,2,32]{2,1,0:T(2,128)}, u32[]{:S(2)}) copy-start(s32[1,2,32]{2,1,0:T(2,128)} %param.20) | copy-start | bytes 772
  10.5 46.2 %all-to-all-start = ((bf16[2,32,4,1024]{3,2,0,1:T(4,128)(2,1)}), bf16[2,32,4,1024]{3,2,0,1:T(4,128)(2,1)S(1)}, u32[]{:S(2)}, u32[]{:S(2)}) async-start(bf16[2,32,4,1024]{3,2,0,1:T(4,128)(2,1)} %pad_maximum_fusion.4), calls=%async_computation | async-start | bytes 1048576 | tf_op jit(solution)/shard_map/all_to_all | solution.py:89
  58.9 39.4 %all-to-all-start.1 = ((bf16[2,1,32,4,1024]{4,3,0,1,2:T(4,128)(2,1)}), bf16[2,1,32,4,1024]{4,3,0,1,2:T(4,128)(2,1)S(1)}, u32[]{:S(2)}, u32[]{:S(2)}) async-start(bf16[2,1,32,4,1024]{4,3,0,1,2:T(4,128)(2,1)} %fusion.71), calls=%async_computation.1 | async-start | bytes 1048576 | tf_op jit(solution)/shard_map/all_to_all | solution.py:93
  69.8 786.9 %all-gather.3.cloned.1.call-start = ((), (), s32[]{:S(2)}) async-start(), calls=%async_computation.7 | async-start | bytes 2101248 | tf_op jit(solution)/shard_map/all_gather | solution.py:72
  70.5 38.5 %copy-start.5 = (bf16[1,1,128,1024]{3,2,1,0:T(8,128)(2,1)S(1)}, bf16[1,1,128,1024]{3,2,1,0:T(8,128)(2,1)}, u32[]{:S(2)}) copy-start(bf16[1,1,128,1024]{3,2,1,0:T(8,128)(2,1)} %param.15) | copy-start | bytes 786436
  71.5 38.3 %copy-start.9 = (s32[1,1,3,1,1]{2,4,3,1,0:T(1,128)S(1)}, s32[1,1,3,1,1]{2,4,3,1,0:T(1,128)}, u32[]{:S(2)}) copy-start(s32[1,1,3,1,1]{2,4,3,1,0:T(1,128)} %param.22) | copy-start | bytes 40
  71.6 38.4 %copy-start.8 = (f32[32,16]{0,1:T(8,128)S(1)}, f32[32,16]{0,1:T(8,128)}, u32[]{:S(2)}) copy-start(f32[32,16]{0,1:T(8,128)} %param.23) | copy-start | bytes 6148
  71.6 38.5 %copy-start.10 = (s32[1,1,2,1,1]{2,4,3,1,0:T(1,128)S(1)}, s32[1,1,2,1,1]{2,4,3,1,0:T(1,128)}, u32[]{:S(2)}) copy-start(s32[1,1,2,1,1]{2,4,3,1,0:T(1,128)} %param.21) | copy-start | bytes 28
  98.4 38.5 %all-to-all-start.2 = ((bf16[2,1,32,4,1024]{4,3,0,1,2:T(4,128)(2,1)}), bf16[2,1,32,4,1024]{4,3,0,1,2:T(4,128)(2,1)S(1)}, u32[]{:S(2)}, u32[]{:S(2)}) async-start(bf16[2,1,32,4,1024]{4,3,0,1,2:T(4,128)(2,1)} %fusion.70), calls=%async_computation.2 | async-start | bytes 1048576 | tf_op jit(solution)/shard_map/all_to_all | solution.py:93
  861.9 4.3 copy-start.11
  864.1 2.2 copy-start.12
  874.5 4.3 copy-start.11
  887.0 4.3 copy-start.11
  889.2 2.2 copy-start.12
  899.5 4.3 copy-start.11
  928.0 27.9 %copy-start.1 = (bf16[2,1,128,1024]{3,0,2,1:T(2,128)(2,1)S(1)}, bf16[2,1,128,1024]{3,0,2,1:T(2,128)(2,1)}, u32[]{:S(2)}) copy-start(bf16[2,1,128,1024]{3,0,2,1:T(2,128)(2,1)} %get-tuple-element.193) | copy-start | bytes 1572868
  947.6 47.0 %copy-start.7 = (s32[1,2,32]{2,1,0:T(2,128)S(1)}, s32[1,2,32]{2,1,0:T(2,128)}, u32[]{:S(2)}) copy-start(s32[1,2,32]{2,1,0:T(2,128)} %param.20) | copy-start | bytes 772
  947.6 36.6 %all-to-all-start.3 = ((bf16[32,2,1,1,4,1024]{5,1,4,3,2,0:T(2,128)(2,1)}), bf16[32,2,1,1,4,1024]{5,1,4,3,2,0:T(2,128)(2,1)S(1)}, u32[]{:S(2)}, u32[]{:S(2)}) async-start(bf16[32,2,1,1,4,1024]{5,1,4,3,2,0:T(2,128)(2,1)} %constant_dynamic-update-slice_fusion), calls=%async_computation.3 | async-start | bytes 1048576 | tf_op jit(solution)/shard_map/all_to_all | solution.py:128
  984.2 39.2 %all-to-all-start.5 = ((bf16[32,2,1,1,4,1024]{5,1,4,3,2,0:T(2,128)(2,1)}), bf16[32,2,1,1,4,1024]{5,1,4,3,2,0:T(2,128)(2,1)S(1)}, u32[]{:S(2)}, u32[]{:S(2)}) async-start(bf16[32,2,1,1,4,1024]{5,1,4,3,2,0:T(2,128)(2,1)} %constant_dynamic-update-slice_fusion.32), calls=%async_computation.5 | async-start | bytes 1048576 | tf_op jit(solution)/shard_map/all_to_all | solution.py:128
  1023.4 38.6 %all-to-all-start.4 = ((bf16[2,1,32,4,1024]{4,0,3,1,2:T(2,128)(2,1)}), bf16[2,1,32,4,1024]{4,0,3,1,2:T(2,128)(2,1)S(1)}, u32[]{:S(2)}, u32[]{:S(2)}) async-start(bf16[2,1,32,4,1024]{4,0,3,1,2:T(2,128)(2,1)} %fusion.72), calls=%async_computation.4 | async-start | bytes 1048576 | tf_op jit(solution)/shard_map/all_to_all | solution.py:131
  1033.7 515.9 %all-reduce.3.cloned.1.call-start = ((), (), s32[]{:S(2)}) async-start(), calls=%async_computation.8 | async-start | bytes 8388608
  1062.0 10.9 copy-start.2
  1062.0 488.9 %all-to-all-start.6 = ((bf16[2,1,32,4,1024]{4,0,3,1,2:T(2,128)(2,1)}), bf16[2,1,32,4,1024]{4,0,3,1,2:T(2,128)(2,1)}, u32[]{:S(2)}, u32[]{:S(2)}) async-start(bf16[2,1,32,4,1024]{4,0,3,1,2:T(2,128)(2,1)} %fusion.73), calls=%async_computation.6 | async-start | bytes 1048576 | tf_op jit(solution)/shard_map/all_to_all | solution.py:131
  (4 other events, 7.0 us)
Sparse Core Ops, SparseCore 0:
  72.7 783.9 all-gather.2
  1040.0 509.5 all-reduce.2
